TPU v7x, 256 devices: a whole 4x4x8 slice. The times are simulated.
256 devices in a mesh: blk: 32 (over x, y, core), sub: 8 (over z).
Axes of the slice: x: 4, y: 4, z: 8, core: 2. Of those that a mesh axis runs over, the one named last changes fastest.
Arguments:
- block_vec: bfloat16 [64, 512, 512], P('blk', 'sub'), may hold values from -6 to 6
- left_factor: bfloat16 [8, 512, 512], replicated, may hold values from -0.25 to 0.25
- right_factor: bfloat16 [8, 512, 512], replicated, may hold values from -0.25 to 0.25
- pairs: int32 [32, 32, 2, 3], replicated, may hold values from 0 to 7, as said below
- pair_count: int32 [32, 32], replicated, may hold values from 1 to 2, as said below
- left_basis: bfloat16 [64, 512, 512], P('blk'), may hold values from -0.25 to 0.25
- left_dual: bfloat16 [64, 512, 512], P('blk'), may hold values from -0.25 to 0.25
- right_eigenvector_matrix: bfloat16 [64, 512, 512], P('blk'), may hold values from -0.25 to 0.25
- right_dual: bfloat16 [64, 512, 512], P('blk'), may hold values from -0.25 to 0.25
- left_rates: float32 [64, 512], P('blk', 'sub'), may hold values from 0.5 to 8
- right_rates: float32 [64, 512], P('blk'), may hold values from 0.5 to 8
Outputs:
- next_vec: float32 [64, 512, 512], P('blk', None, 'sub')
Inputs may be any that keep to these rules, and one draw needn't show every extreme that they name: `pairs`: entry [g, h, c, 0] is a source block index within group g, [g, h, c, 1] a target block index within group h (0 to 1), and [g, h, c, 2] a term index (0 to 7); where g equals h, source and target differ. For some target group h, pair_count[g, h] is 2 for every g.
All inputs are finite; a program needn't handle non-finite values.
Results may differ from a plain program's by a relative error of at most 0.023.
Values may be sent and summed in bfloat16 or wider, within the bound.
No kernel may reach another device: no remote copies, remote signals or barrier semaphores. Data moves between devices by JAX's collectives and lax.ppermute only.
A program may use at most 64 MiB of HBM per device.

v0:
```python
import jax
import jax.numpy as jnp
from jax import lax
from jax.sharding import PartitionSpec as P


def local(
    block_vec,
    left_factor,
    right_factor,
    pairs,
    pair_count,
    left_basis,
    left_dual,
    right_eigenvector_matrix,
    right_dual,
    left_rates,
    right_rates,
):
    owner = lax.axis_index("blk")
    groups = lax.axis_size("blk")
    local_blocks = block_vec.shape[0]
    row_count = block_vec.shape[1]
    width_two = block_vec.shape[2]
    slots_per = pairs.shape[2]
    term_total = left_factor.shape[0]
    all_count = groups * local_blocks
    incoming = lax.dynamic_index_in_dim(pairs, owner, 1, keepdims=False)
    counts = lax.dynamic_index_in_dim(pair_count, owner, 1, keepdims=False)
    live_mask = (jnp.arange(slots_per)[None, :] < counts[:, None]).astype(jnp.float32)
    target_term = incoming[..., 1] * term_total + incoming[..., 2]
    source = jnp.arange(groups, dtype=jnp.int32)[:, None] * local_blocks + incoming[..., 0]
    key_onehot = (
        target_term[..., None] == jnp.arange(local_blocks * term_total)[None, None, :]
    ).astype(jnp.float32) * live_mask[..., None]
    source_onehot = (source[..., None] == jnp.arange(all_count)[None, None, :]).astype(jnp.float32)
    weights = jnp.einsum("gqk,gqs->ks", key_onehot, source_onehot).astype(jnp.bfloat16)
    everything = lax.all_gather(block_vec, "blk", axis=0, tiled=True)
    pooled = jnp.einsum(
        "ks,srn->krn", weights, everything, preferred_element_type=jnp.float32
    ).astype(jnp.bfloat16)
    pooled = pooled.reshape(local_blocks, term_total, row_count, width_two)
    right_done = jnp.einsum(
        "ktrn,tmn->ktrm", pooled, right_factor, preferred_element_type=jnp.float32
    ).astype(jnp.bfloat16)
    right_cols = lax.all_to_all(right_done, "sub", split_axis=3, concat_axis=2, tiled=True)
    summed = jnp.einsum(
        "tab,ktbc->kac", left_factor, right_cols, preferred_element_type=jnp.float32
    ).astype(jnp.bfloat16)
    dual_cols = jnp.einsum(
        "jab,jbc->jac", left_dual, summed, preferred_element_type=jnp.float32
    ).astype(jnp.bfloat16)
    dual_rows = lax.all_to_all(dual_cols, "sub", split_axis=1, concat_axis=2, tiled=True)
    mixed = jnp.einsum("jrn,jmn->jrm", dual_rows, right_dual, preferred_element_type=jnp.float32)
    scaled = (mixed / (left_rates[:, :, None] + right_rates[:, None, :])).astype(jnp.bfloat16)
    basis_rows = jnp.einsum(
        "jrm,jkm->jrk", scaled, right_eigenvector_matrix, preferred_element_type=jnp.float32
    ).astype(jnp.bfloat16)
    basis_cols = lax.all_to_all(basis_rows, "sub", split_axis=2, concat_axis=1, tiled=True)
    return jnp.einsum("jab,jbc->jac", left_basis, basis_cols, preferred_element_type=jnp.float32)


def solution(mesh):
    placed = (
        P("blk", "sub", None),
        P(),
        P(),
        P(),
        P(),
        P("blk", None, None),
        P("blk", None, None),
        P("blk", None, None),
        P("blk", None, None),
        P("blk", "sub"),
        P("blk", None),
    )
    return jax.shard_map(
        local, mesh=mesh, in_specs=placed, out_specs=P("blk", None, "sub"), check_vma=False
    )
```

profile of v0, /device:TPU:2, one launch (start us, length us, event | category | flops | bytes accessed | tf_op | source)
XLA Modules:
  0.0 167.2 jit_solution(14784271772205998171)
XLA Ops:
  6.5 0.7 all-gather.2.cloned.1.call-update
  7.3 1.1 constant_dynamic-slice_fusion
  8.3 0.1 copy.25
  8.4 0.9 dynamic-slice_reduce_fusion
  9.4 54.3 %all-gather.2.cloned.1.call-done = bf16[64,64,512]{2,1,0:T(8,128)(2,1)} async-done(((bf16[2,64,512]{2,1,0:T(8,128)(2,1)}), bf16[64,64,512]{2,1,0:T(8,128)(2,1)}) %all-gather.2.cloned.1.call-update) | async-done | bytes 4194320 | tf_op jit(solution)/shard_map/all_gather | solution.py:38
  63.7 6.7 %fusion.15 = bf16[2,8,64,512]{3,1,0,2:T(8,128)(2,1)S(1)} fusion(bf16[64,64,512]{2,1,0:T(8,128)(2,1)} %all-gather.2.cloned.1.call-done, s32[32,2]{0,1:T(2,128)S(1)} %get-tuple-element.6, bf16[32,2]{0,1:T(2,128)(2,1)S(1)} %compare_convert_fusion, s32[32,2]{0,1:T(2,128)S(1)} %get-tuple-element.5), kind=kOutput, calls=%fused_computation.10 | convolution fusion | flops 67770368 | bytes 5243520 | tf_op jit(solution)/shard_map/ks,srn->krn/dot_general | solution.py:39
  70.4 4.8 %fusion.12 = bf16[2,8,64,512]{3,2,0,1:T(8,128)(2,1)} fusion(bf16[8,512,512]{2,1,0:T(8,128)(2,1)} %param.13, bf16[2,8,64,512]{3,1,0,2:T(8,128)(2,1)S(1)} %fusion.15), kind=kOutput, calls=%fused_computation.9 | convolution fusion | flops 537395200 | bytes 6291456 | tf_op jit(solution)/shard_map/ktrn,tmn->ktrm/dot_general | solution.py:43
  75.2 4.7 %copy.28 = bf16[2,8,64,512]{2,0,1,3:T(2,128)(2,1)S(1)} copy(bf16[2,8,64,512]{3,2,0,1:T(8,128)(2,1)} %fusion.12) | data formatting | bytes 2097152 | tf_op jit(solution)/shard_map/convert_element_type | solution.py:45
  80.0 2.7 %reshape.46 = bf16[8,2,32768]{2,1,0:T(2,128)(2,1)} reshape(bf16[512,8,2,64]{3,2,1,0:T(2,128)(2,1)S(1)} %bitcast.85) | data formatting | bytes 2097152
  82.6 36.3 %all_to_all.54 = bf16[8,2,32768]{2,1,0:T(2,128)(2,1)} all-to-all(bf16[8,2,32768]{2,1,0:T(2,128)(2,1)} %reshape.46), channel_id=1, replica_groups=mesh['blk'=32,'sub'=8] {'sub'}, dimensions={0} | all-to-all | bytes 2097152 | tf_op jit(solution)/shard_map/all_to_all | solution.py:46
  118.9 3.1 %reshape.47 = bf16[512,8,2,64]{3,2,1,0:T(2,128)(2,1)S(1)} reshape(bf16[8,2,32768]{2,1,0:T(2,128)(2,1)} %all_to_all.54) | data formatting | bytes 2097152
  122.0 2.7 %copy.47 = bf16[2,8,64,8,64]{2,3,4,1,0:T(8,128)(2,1)} copy(bf16[2,8,64,8,64]{2,0,1,4,3:T(2,128)(2,1)S(1)} %bitcast.86) | data formatting | bytes 2097152 | tf_op jit(solution)/shard_map/all_to_all | solution.py:46
  124.7 3.2 %all_to_all.42 = bf16[2,8,512,64]{2,3,1,0:T(8,128)(2,1)S(1)} reshape(bf16[2,8,8,64,64]{3,2,4,1,0:T(8,128)(2,1)} %bitcast.87) | data formatting | bytes 2097152 | tf_op jit(solution)/shard_map/all_to_all | solution.py:46
  127.9 0.0 copy-start.2
  127.9 0.0 copy-start.3
  127.9 4.0 %fusion.25 = bf16[2,512,64]{1,2,0:T(8,128)(2,1)S(1)} fusion(bf16[2,512,512]{2,1,0:T(8,128)(2,1)S(1)} %copy-done, bf16[2,8,512,64]{2,3,1,0:T(8,128)(2,1)S(1)} %all_to_all.42, bf16[8,512,512]{2,1,0:T(8,128)(2,1)} %param.12), kind=kOutput, calls=%fused_computation.18 | convolution fusion | flops 604110848 | bytes 6422528 | tf_op jit(solution)/shard_map/jab,jbc->jac/dot_general | solution.py:50
  131.9 0.0 copy-start.1
  131.9 0.2 copy.30
  132.1 0.2 reshape.48
  132.3 11.5 %all_to_all.55 = bf16[8,2,4096]{2,1,0:T(2,128)(2,1)S(1)} all-to-all(bf16[8,2,4096]{2,1,0:T(2,128)(2,1)S(1)} %reshape.48), channel_id=1, replica_groups=mesh['blk'=32,'sub'=8] {'sub'}, dimensions={0} | all-to-all | bytes 262144 | tf_op jit(solution)/shard_map/all_to_all | solution.py:53
  143.8 0.2 reshape.49
  144.0 0.2 copy.49
  144.2 0.2 all_to_all.46
  144.4 0.0 copy-done.2
  144.4 2.3 %convolution_convert_fusion = bf16[2,64,512]{2,1,0:T(8,128)(2,1)S(1)} fusion(bf16[2,512,512]{2,1,0:T(8,128)(2,1)} %param.18, bf16[2,64,512]{2,1,0:T(8,128)(2,1)S(1)} %all_to_all.46, bf16[2,512,512]{2,1,0:T(8,128)(2,1)} %param.19, f32[2,512]{1,0:T(2,128)S(1)} %copy-done.2, f32[2,64]{1,0:T(2,128)S(1)} %copy-done.3), kind=kOutput, calls=%fused_computation.15 | convolution fusion | flops 134479872 | bytes 2363904 | tf_op jit(solution)/shard_map/jrm,jkm->jrk/dot_general | solution.py:56
  146.7 0.2 copy.32
  146.9 0.2 reshape.50
  147.1 11.5 %all_to_all.56 = bf16[8,2,4096]{2,1,0:T(2,128)(2,1)S(1)} all-to-all(bf16[8,2,4096]{2,1,0:T(2,128)(2,1)S(1)} %reshape.50), channel_id=1, replica_groups=mesh['blk'=32,'sub'=8] {'sub'}, dimensions={0} | all-to-all | bytes 262144 | tf_op jit(solution)/shard_map/all_to_all | solution.py:59
  158.6 0.2 reshape.51
  158.8 0.2 copy.48
  159.0 0.2 all_to_all.50
  159.2 1.1 convolution_bitcast_fusion
  (8 shorter events, 0.0 us)
Async XLA Ops:
  6.5 121.3 %copy-start = (bf16[2,512,512]{2,1,0:T(8,128)(2,1)S(1)}, bf16[2,512,512]{2,1,0:T(8,128)(2,1)}, u32[]{:S(2)}) copy-start(bf16[2,512,512]{2,1,0:T(8,128)(2,1)} %param.17) | copy-start | bytes 3145732
  6.5 57.1 %all-gather.2.cloned.1.call-start = ((), (), s32[]{:S(2)}) async-start(), calls=%async_computation.3 | async-start | bytes 4325376 | tf_op jit(solution)/shard_map/all_gather | solution.py:38
  127.9 16.5 %copy-start.2 = (f32[2,512]{1,0:T(2,128)S(1)}, f32[2,512]{1,0:T(2,128)}, u32[]{:S(2)}) copy-start(f32[2,512]{1,0:T(2,128)} %param.21) | copy-start | bytes 12292
  127.9 16.5 %copy-start.3 = (f32[2,64]{1,0:T(2,128)S(1)}, f32[2,64]{1,0:T(2,128)}, u32[]{:S(2)}) copy-start(f32[2,64]{1,0:T(2,128)} %param.20) | copy-start | bytes 1540
  131.9 27.3 %copy-start.1 = (bf16[2,512,512]{2,1,0:T(8,128)(2,1)S(1)}, bf16[2,512,512]{2,1,0:T(8,128)(2,1)}, u32[]{:S(2)}) copy-start(bf16[2,512,512]{2,1,0:T(8,128)(2,1)} %param.16) | copy-start | bytes 3145732
Sparse Core Ops, SparseCore 0:
  9.9 53.7 all-gather.1
where the time goes:
time: 168 us; the launch traced here: 167 us
  blocking collectives  59.2 us (35%)
  waiting for transfers between devices  55 us (33%)
  local copies, waits for them, and re-layouts  20.5 us (12%)
  matrix products  19 us (11%)
  between operations  13.6 us (8%)
    all_gather x1, waiting for transfers between devices, local(): everything = lax.all_gather(block_vec, 'blk', axis=0, tiled=True)  54.3 us
    all_to_all x1, blocking collectives, local(): lax.all_to_all(right_done, 'sub', split_axis=3, concat_axis=2, tiled=True)  36.3 us
    all_to_all x1, blocking collectives, local(): lax.all_to_all(dual_cols, 'sub', split_axis=1, concat_axis=2, tiled=True)  11.5 us
    all_to_all x1, blocking collectives, local(): lax.all_to_all(basis_rows, 'sub', split_axis=2, concat_axis=1, tiled=True)  11.5 us
    dot_general x1, matrix products, local(): jnp.einsum('ks,srn->krn', weights, everything, preferred_element_type=jnp...  6.75 us
    unnamed x14, local copies, waits for them, and re-layouts  6.67 us
    all_to_all x2, local copies, waits for them, and re-layouts, local(): lax.all_to_all(right_done, 'sub', split_axis=3, concat_axis=2, tiled=True)  5.88 us
    dot_general x1, matrix products, local(): jnp.einsum('ktrn,tmn->ktrm', pooled, right_factor, preferred_element_type...  4.8 us
  transfers between devices with their start and end apart: 1, of which 1 were waited for; matrix products, arithmetic and copies ran while one was open for 1% of the time, Pallas kernels for 0%

commit v1 on v0

--- a/solution.py
+++ b/solution.py
@@ -2,6 +2,12 @@
 import jax.numpy as jnp
 from jax import lax
 from jax.sharding import PartitionSpec as P
+
+
+def swap_blocks(array, name, split, join):
+    parts = jnp.split(array, lax.axis_size(name), axis=split)
+    arrived = lax.all_to_all(jnp.stack(parts), name, 0, 0)
+    return jnp.concatenate(arrived, axis=join)
 
 
 def local(
@@ -43,7 +49,7 @@
     right_done = jnp.einsum(
         "ktrn,tmn->ktrm", pooled, right_factor, preferred_element_type=jnp.float32
     ).astype(jnp.bfloat16)
-    right_cols = lax.all_to_all(right_done, "sub", split_axis=3, concat_axis=2, tiled=True)
+    right_cols = swap_blocks(right_done, "sub", 3, 2)
     summed = jnp.einsum(
         "tab,ktbc->kac", left_factor, right_cols, preferred_element_type=jnp.float32
     ).astype(jnp.bfloat16)

time: 168 us -> 166 us (0.988)
    reshape x0 -> x3, local copies, waits for them, and re-layouts: none -> 6.82 us  [swap_blocks(): return jnp.concatenate(arrived, axis=join)]
    all_to_all x2 -> x0, local copies, waits for them, and re-layouts: 5.88 us -> none  [local(): lax.all_to_all(right_done, 'sub', split_axis=3, concat_axis=2, tiled=True)]
    convert_element_type x1 -> x0, local copies, waits for them, and re-layouts: 4.74 us -> none  [local(): right_done = jnp.einsum('ktrn,tmn->ktrm', pooled, right_factor, preferred...]
    unnamed x14 -> x25, local copies, waits for them, and re-layouts: 6.67 us -> 9.54 us
where the time goes in v1:
time: 166 us; the launch traced here: 165 us
  blocking collectives  59 us (36%)
  waiting for transfers between devices  55 us (33%)
  local copies, waits for them, and re-layouts  19.7 us (12%)
  matrix products  18.1 us (11%)
  between operations  13.6 us (8%)
    all_gather x1, waiting for transfers between devices, local(): everything = lax.all_gather(block_vec, 'blk', axis=0, tiled=True)  54.3 us
    all_to_all x1, blocking collectives, swap_blocks(): arrived = lax.all_to_all(jnp.stack(parts), name, 0, 0)  36.1 us
    all_to_all x1, blocking collectives, local(): lax.all_to_all(dual_cols, 'sub', split_axis=1, concat_axis=2, tiled=True)  11.5 us
    all_to_all x1, blocking collectives, local(): lax.all_to_all(basis_rows, 'sub', split_axis=2, concat_axis=1, tiled=True)  11.5 us
    unnamed x25, local copies, waits for them, and re-layouts  9.54 us
    reshape x3, local copies, waits for them, and re-layouts, swap_blocks(): return jnp.concatenate(arrived, axis=join)  6.82 us
    dot_general x1, matrix products, local(): jnp.einsum('ks,srn->krn', weights, everything, preferred_element_type=jnp...  6.75 us
    dot_general x1, matrix products, local(): jnp.einsum('jab,jbc->jac', left_dual, summed, preferred_element_type=jnp....  4.3 us
  transfers between devices with their start and end apart: 1, of which 1 were waited for; matrix products, arithmetic and copies ran while one was open for 1% of the time, Pallas kernels for 0%

profile of v1, /device:TPU:2, one launch (start us, length us, event | category | flops | bytes accessed | tf_op | source)
XLA Modules:
  0.0 165.5 jit_solution(5505794938168404843)
XLA Ops:
  6.5 0.7 all-gather.2.cloned.1.call-update
  7.3 1.1 constant_dynamic-slice_fusion
  8.4 0.9 dynamic-slice_reduce_fusion
  9.4 54.3 %all-gather.2.cloned.1.call-done = bf16[64,64,512]{2,1,0:T(8,128)(2,1)} async-done(((bf16[2,64,512]{2,1,0:T(8,128)(2,1)}), bf16[64,64,512]{2,1,0:T(8,128)(2,1)}) %all-gather.2.cloned.1.call-update) | async-done | bytes 4194320 | tf_op jit(solution)/shard_map/all_gather | solution.py:44
  63.7 6.7 %fusion.15 = bf16[2,8,64,512]{3,1,0,2:T(8,128)(2,1)S(1)} fusion(bf16[64,64,512]{2,1,0:T(8,128)(2,1)} %all-gather.2.cloned.1.call-done, s32[32,2]{0,1:T(2,128)S(1)} %get-tuple-element.6, bf16[32,2]{0,1:T(2,128)(2,1)S(1)} %compare_convert_fusion, s32[32,2]{0,1:T(2,128)S(1)} %get-tuple-element.5), kind=kOutput, calls=%fused_computation.9 | convolution fusion | flops 67770368 | bytes 5243520 | tf_op jit(solution)/shard_map/ks,srn->krn/dot_general | solution.py:45
  70.4 3.8 %fusion.12 = bf16[2,8,64,512]{3,2,0,1:T(8,128)(2,1)S(1)} fusion(bf16[8,512,512]{2,1,0:T(8,128)(2,1)} %param.13, bf16[2,8,64,512]{3,1,0,2:T(8,128)(2,1)S(1)} %fusion.15), kind=kOutput, calls=%fused_computation.8 | convolution fusion | flops 537395200 | bytes 6291456 | tf_op jit(solution)/shard_map/ktrn,tmn->ktrm/dot_general | solution.py:49
  74.3 0.2 fusion.37
  74.6 0.2 fusion.35
  74.8 0.2 fusion.33
  75.1 0.2 fusion.31
  75.3 1.3 copy-done.1
  76.7 3.4 %reshape.54 = bf16[8,2,32768]{2,1,0:T(2,128)(2,1)S(1)} reshape(bf16[8,8,2,64,64]{4,3,2,1,0:T(8,128)(2,1)} %bitcast.116) | data formatting | bytes 2097152
  80.0 36.1 %all_to_all.41 = bf16[8,2,32768]{2,1,0:T(2,128)(2,1)} all-to-all(bf16[8,2,32768]{2,1,0:T(2,128)(2,1)S(1)} %reshape.54), channel_id=1, replica_groups=mesh['blk'=32,'sub'=8] {'sub'}, dimensions={0} | all-to-all | bytes 2097152 | tf_op jit(solution)/shard_map/all_to_all | solution.py:9
  116.1 3.1 %reshape.55 = bf16[8,8,2,64,64]{4,3,2,1,0:T(8,128)(2,1)S(1)} reshape(bf16[8,2,32768]{2,1,0:T(2,128)(2,1)} %all_to_all.41) | data formatting | bytes 2097152
  119.2 1.5 bitcast_bitcast_fusion
  120.7 3.2 %copy.28 = bf16[2,8,8,64,64]{3,2,4,1,0:T(8,128)(2,1)S(1)} copy(bf16[2,8,8,64,64]{4,3,0,1,2:T(8,128)(2,1)} %bitcast_bitcast_fusion) | data formatting | bytes 2097152 | tf_op jit(solution)/shard_map/reshape | solution.py:10
  124.0 2.0 %reshape.47 = bf16[2,8,512,64]{2,3,1,0:T(8,128)(2,1)} reshape(bf16[2,8,8,64,64]{3,2,4,1,0:T(8,128)(2,1)S(1)} %copy.28) | data formatting | bytes 2097152 | tf_op jit(solution)/shard_map/reshape | solution.py:10
  126.0 4.3 %fusion.25 = bf16[2,512,64]{1,2,0:T(8,128)(2,1)S(1)} fusion(bf16[2,512,512]{2,1,0:T(8,128)(2,1)S(1)} %copy-done, bf16[2,8,512,64]{2,3,1,0:T(8,128)(2,1)} %reshape.47, bf16[8,512,512]{2,1,0:T(8,128)(2,1)} %param.12), kind=kOutput, calls=%fused_computation.17 | convolution fusion | flops 604110848 | bytes 6422528 | tf_op jit(solution)/shard_map/jab,jbc->jac/dot_general | solution.py:56
  130.4 0.2 copy.29
  130.5 0.2 reshape.56
  130.8 11.5 %all_to_all.42 = bf16[8,2,4096]{2,1,0:T(2,128)(2,1)S(1)} all-to-all(bf16[8,2,4096]{2,1,0:T(2,128)(2,1)S(1)} %reshape.56), channel_id=1, replica_groups=mesh['blk'=32,'sub'=8] {'sub'}, dimensions={0} | all-to-all | bytes 262144 | tf_op jit(solution)/shard_map/all_to_all | solution.py:59
  142.2 0.2 reshape.57
  142.5 0.2 copy.46
  142.6 0.2 all_to_all.33
  142.9 2.1 %convolution_convert_fusion = bf16[2,64,512]{2,1,0:T(8,128)(2,1)S(1)} fusion(bf16[2,512,512]{2,1,0:T(8,128)(2,1)S(1)} %copy-done.3, bf16[2,64,512]{2,1,0:T(8,128)(2,1)S(1)} %all_to_all.33, bf16[2,512,512]{2,1,0:T(8,128)(2,1)} %param.19, f32[2,512]{1,0:T(2,128)S(1)} %copy-done.4, f32[2,64]{1,0:T(2,128)S(1)} %copy-done.5), kind=kOutput, calls=%fused_computation.14 | convolution fusion | flops 134479872 | bytes 2363904 | tf_op jit(solution)/shard_map/jrm,jkm->jrk/dot_general | solution.py:62
  145.0 0.2 copy.31
  145.1 0.2 reshape.58
  145.4 11.5 %all_to_all.43 = bf16[8,2,4096]{2,1,0:T(2,128)(2,1)S(1)} all-to-all(bf16[8,2,4096]{2,1,0:T(2,128)(2,1)S(1)} %reshape.58), channel_id=1, replica_groups=mesh['blk'=32,'sub'=8] {'sub'}, dimensions={0} | all-to-all | bytes 262144 | tf_op jit(solution)/shard_map/all_to_all | solution.py:65
  156.8 0.2 reshape.59
  157.1 0.2 copy.45
  157.2 0.2 all_to_all.37
  157.5 1.1 convolution_bitcast_fusion
  (20 shorter events, 0.4 us)
Async XLA Ops:
  6.5 119.5 %copy-start = (bf16[2,512,512]{2,1,0:T(8,128)(2,1)S(1)}, bf16[2,512,512]{2,1,0:T(8,128)(2,1)}, u32[]{:S(2)}) copy-start(bf16[2,512,512]{2,1,0:T(8,128)(2,1)} %param.17) | copy-start | bytes 3145732
  6.5 57.1 %all-gather.2.cloned.1.call-start = ((), (), s32[]{:S(2)}) async-start(), calls=%async_computation.3 | async-start | bytes 4325376 | tf_op jit(solution)/shard_map/all_gather | solution.py:44
  75.3 1.4 copy-start.1
  130.3 12.5 %copy-start.3 = (bf16[2,512,512]{2,1,0:T(8,128)(2,1)S(1)}, bf16[2,512,512]{2,1,0:T(8,128)(2,1)}, u32[]{:S(2)}) copy-start(bf16[2,512,512]{2,1,0:T(8,128)(2,1)} %param.18) | copy-start | bytes 3145732
  130.3 12.5 %copy-start.4 = (f32[2,512]{1,0:T(2,128)S(1)}, f32[2,512]{1,0:T(2,128)}, u32[]{:S(2)}) copy-start(f32[2,512]{1,0:T(2,128)} %param.21) | copy-start | bytes 12292
  130.3 12.5 %copy-start.5 = (f32[2,64]{1,0:T(2,128)S(1)}, f32[2,64]{1,0:T(2,128)}, u32[]{:S(2)}) copy-start(f32[2,64]{1,0:T(2,128)} %param.20) | copy-start | bytes 1540
  142.9 14.6 %copy-start.2 = (bf16[2,512,512]{2,1,0:T(8,128)(2,1)S(1)}, bf16[2,512,512]{2,1,0:T(8,128)(2,1)}, u32[]{:S(2)}) copy-start(bf16[2,512,512]{2,1,0:T(8,128)(2,1)} %param.16) | copy-start | bytes 3145732
Sparse Core Ops, SparseCore 0:
  9.9 53.7 all-gather.1
